TPU v7x, 256 devices: a whole 4x4x8 slice. The times are simulated.
256 devices in a mesh: prow: 16 (over z, core), pcol: 16 (over y, x).
Axes of the slice: x: 4, y: 4, z: 8, core: 2. Of those that a mesh axis runs over, the one named last changes fastest.
Arguments:
- kernel: float32 [3, 16, 256, 3, 16, 256], P(None, 'prow', None, None, 'pcol'), as said below
Outputs:
- factored: float32 [3, 16, 256, 3, 16, 256], P(None, 'prow', None, None, 'pcol')
Inputs may be any that keep to these rules, and one draw needn't show every extreme that they name: kernel is symmetric (entry (a, b) equals entry (b, a)); every diagonal entry is 1.1, every off-diagonal entry lies in (0, 1], and the matrix is positive definite with smallest eigenvalue at least 0.1.
All inputs are finite; a program needn't handle non-finite values.
Results may differ from a plain program's by a relative error of at most 0.0003.
Values sent between devices are 32-bit elements; how exact they have to be, the bound alone decides.
No kernel may reach another device: no remote copies, remote signals or barrier semaphores. Data moves between devices by JAX's collectives and lax.ppermute only.
A program may use at most 64 MiB of HBM per device.

v0:
```python
import jax
import jax.numpy as jnp
from jax import lax
from jax.sharding import PartitionSpec as P

HIGH = lax.Precision.HIGHEST


def chol_and_inverse(block, eye):
    h = block.shape[0] // 2
    small = eye[:h, :h]
    la = jnp.linalg.cholesky(block[:h, :h], symmetrize_input=False)
    wa = jax.scipy.linalg.solve_triangular(la, small, lower=True)
    lb = jnp.dot(block[h:, :h], wa.T, precision=HIGH)
    lc = jnp.linalg.cholesky(
        block[h:, h:] - jnp.dot(lb, lb.T, precision=HIGH), symmetrize_input=False
    )
    wc = jax.scipy.linalg.solve_triangular(lc, small, lower=True)
    wb = -jnp.dot(wc, jnp.dot(lb, wa, precision=HIGH), precision=HIGH)
    zero = jnp.zeros_like(small)
    lower = jnp.block([[la, zero], [lb, lc]])
    inverse = jnp.block([[wa, zero], [wb, wc]])
    return lower, inverse


def from_two_sources(own, axis, sources):
    peers = lax.axis_size(axis)
    shape = own.shape
    flat = own.reshape(-1, shape[-1])
    spare = -flat.shape[0] % peers
    flat = jnp.pad(flat, [(0, spare), (0, 0)])
    pieces = flat.reshape(peers, -1, shape[-1])
    mine = lax.all_to_all(pieces, axis, 0, 0, tiled=False)
    kept = jnp.stack([mine[s] for s in sources])
    spread = lax.all_to_all(
        jnp.broadcast_to(kept[None], (peers, *kept.shape)), axis, 0, 0, tiled=False
    )
    whole = jnp.swapaxes(spread, 0, 1).reshape(len(sources), -1, shape[-1])
    whole = whole[:, : flat.shape[0] - spare]
    return whole.reshape(len(sources), *shape)


def on_device(kernel):
    prow = lax.axis_index("prow")
    pcol = lax.axis_index("pcol")
    rows = lax.axis_size("prow")
    cols = lax.axis_size("pcol")
    lbr, blk, lbc = kernel.shape[0], kernel.shape[2], kernel.shape[3]
    work = kernel.reshape(lbr, blk, lbc, blk)
    eye = jnp.eye(blk, dtype=jnp.float32)

    top = work[0]
    top_first = top[:, 0, :].reshape(rows, -1, blk)
    top_rest = jnp.swapaxes(top[:, 1:, :], 0, 1).reshape(rows, -1, blk)
    split = top_first.shape[1]
    top_mine = lax.all_to_all(
        jnp.concatenate([top_first, top_rest], axis=1), "prow", 0, 0, tiled=False
    )
    top_kept = jnp.stack([top_mine[0], top_mine[1]])
    top_spread = lax.all_to_all(
        jnp.broadcast_to(top_kept[None, :, :split], (rows, 2, split, blk)),
        "prow", 0, 0, tiled=False,
    )
    y_first = jnp.swapaxes(top_spread, 0, 1).reshape(2, blk, blk)
    y0c = y_first[0]
    y1c = y_first[1]
    top_gathered = lax.all_gather(top_kept[:, split:], "prow", axis=0, tiled=False)
    y_rest = jnp.swapaxes(top_gathered, 0, 1).reshape(2, lbc - 1, blk, blk)
    ytop = jnp.concatenate([y_first[:, None], y_rest], axis=1).transpose(0, 2, 1, 3)

    extra = jnp.where(pcol == 0, jnp.stack([y0c, y1c]), jnp.stack([y1c, jnp.zeros_like(y1c)]))
    panel = work[:, :, 0, :].reshape(cols, -1, blk)
    extra_pieces = extra.reshape(cols, -1, blk)
    cut = panel.shape[1]
    pieces = jnp.concatenate([panel, extra_pieces], axis=1)
    mine = lax.all_to_all(pieces, "pcol", 0, 0, tiled=False)
    kept = jnp.stack([mine[0], mine[1]])
    spread = lax.all_to_all(
        jnp.broadcast_to(kept[None, :, cut:], (cols, 2, kept.shape[1] - cut, blk)),
        "pcol", 0, 0, tiled=False,
    )
    corner = jnp.swapaxes(spread, 0, 1).reshape(2, 2, blk, blk)
    m00 = corner[0, 0]
    m10 = corner[0, 1]
    m11 = corner[1, 0]
    gathered = lax.all_gather(kept[:, :cut], "pcol", axis=0, tiled=False)
    xs = jnp.swapaxes(gathered, 0, 1).reshape(2, lbr, blk, blk)
    x0 = xs[0]
    x1 = xs[1]

    def factor_step(k, carry):
        block, lowers, inverses, panels = carry
        lower, inverse = chol_and_inverse(block, eye)
        panel = jnp.dot(m10, inverse.T, precision=HIGH)
        nxt = m11 - jnp.dot(panel, panel.T, precision=HIGH)
        return (
            nxt,
            lowers.at[k].set(lower),
            inverses.at[k].set(inverse),
            panels.at[k].set(panel),
        )

    stacked = jnp.zeros((2, blk, blk), jnp.float32)
    _, lowers, inverses, panels = lax.fori_loop(
        0, 2, factor_step, (m00, stacked, stacked, stacked)
    )
    l0, w0, p10 = lowers[0], inverses[0], panels[0]
    l1, w1 = lowers[1], inverses[1]

    r0 = jnp.einsum("aik,jk->aij", x0, w0, precision=HIGH)
    r1 = x1 - jnp.einsum("aik,jk->aij", r0, p10, precision=HIGH)
    r1 = jnp.einsum("aik,jk->aij", r1, w1, precision=HIGH)

    c0t = jnp.einsum("ik,kbj->bij", w0, ytop[0], precision=HIGH)
    c1t = jnp.transpose(ytop[1], (1, 0, 2)) - jnp.einsum(
        "ik,bkj->bij", p10, c0t, precision=HIGH
    )
    c1t = jnp.einsum("ik,bkj->bij", w1, c1t, precision=HIGH)

    left = jnp.concatenate([r0, r1], axis=2)
    right = jnp.concatenate([c0t, c1t], axis=1)
    trailing = work - jnp.einsum("aik,bkj->aibj", left, right, precision=HIGH)

    row_ids = jnp.arange(lbr, dtype=jnp.int32) * rows + prow
    col_ids = jnp.arange(lbc, dtype=jnp.int32) * cols + pcol
    rk = row_ids[:, None, None]
    col0 = jnp.where(rk == 0, l0[None], r0)
    col1 = jnp.where(rk == 0, 0.0, jnp.where(rk == 1, l1[None], r1))
    first_col = jnp.where(pcol == 0, col0, jnp.where(pcol == 1, col1, trailing[:, :, 0, :]))
    out = trailing.at[:, :, 0, :].set(first_col)
    upper = (prow < 2) & (col_ids > prow)
    out = out.at[0].set(jnp.where(upper[None, :, None], 0.0, out[0]))
    return out.reshape(kernel.shape)


def solution(mesh):
    spec = P(None, "prow", None, None, "pcol", None)
    return jax.shard_map(
        on_device, mesh=mesh, in_specs=(spec,), out_specs=spec, check_vma=False
    )
```

profile of v0, /device:TPU:1, one launch (start us, length us, event | category | flops | bytes accessed | tf_op | source)
XLA Modules:
  0.0 246.1 jit_solution(9865918569479223622)
XLA Ops:
  7.4 1.1 slice-done
  8.7 32.7 %all_to_all.20 = f32[16,48,256]{2,1,0:T(8,128)S(1)} all-to-all(f32[16,48,256]{2,1,0:T(8,128)S(1)} %pad_maximum_fusion.1), channel_id=1, replica_groups=mesh['prow'=16,'pcol'=16] {'prow'}, dimensions={0} | all-to-all | bytes 1572864 | tf_op jit(solution)/shard_map/all_to_all | solution.py:56
  43.2 3.5 %all-to-all-start.1 = ((f32[16,2,16,256]{3,2,1,0:T(8,128)}), f32[16,2,16,256]{3,2,1,0:T(8,128)S(1)}, u32[]{:S(2)}, u32[]{:S(2)}) async-start(f32[16,2,16,256]{3,2,1,0:T(8,128)} %broadcast_in_dim.75), calls=%async_computation.1 | async-start | bytes 1048576 | tf_op jit(solution)/shard_map/all_to_all | solution.py:60
  46.7 5.5 %copy.49 = f32[3,1,256,3,1,256]{2,5,0,3,4,1:T(8,128)S(1)} copy(f32[3,1,256,3,1,256]{5,4,3,2,1,0:T(1,128)} %param.16) | data formatting | bytes 4718592 | tf_op args[0]
  52.2 1.0 slice.315
  53.2 2.3 copy.50
  55.5 7.9 %all-to-all-done.1 = f32[16,2,16,256]{3,2,1,0:T(8,128)S(1)} async-done(((f32[16,2,16,256]{3,2,1,0:T(8,128)}), f32[16,2,16,256]{3,2,1,0:T(8,128)S(1)}, u32[]{:S(2)}, u32[]{:S(2)}) %all-to-all-start.1) | async-done | bytes 524320 | tf_op jit(solution)/shard_map/all_to_all | solution.py:60
  63.5 1.2 pad_maximum_fusion
  64.7 6.8 %all-to-all-start.2 = ((f32[16,80,256]{2,1,0:T(8,128)}), f32[16,80,256]{2,1,0:T(8,128)S(1)}, u32[]{:S(2)}, u32[]{:S(2)}) async-start(f32[16,80,256]{2,1,0:T(8,128)} %pad_maximum_fusion), calls=%async_computation.2 | async-start | bytes 2621440 | tf_op jit(solution)/shard_map/all_to_all | solution.py:76
  71.5 1.5 slice.328
  73.0 21.5 %all-to-all-done.2 = f32[16,80,256]{2,1,0:T(8,128)S(1)} async-done(((f32[16,80,256]{2,1,0:T(8,128)}), f32[16,80,256]{2,1,0:T(8,128)S(1)}, u32[]{:S(2)}, u32[]{:S(2)}) %all-to-all-start.2) | async-done | bytes 1310752 | tf_op jit(solution)/shard_map/all_to_all | solution.py:76
  94.5 1.2 broadcast_in_dim.76
  95.9 3.7 %all-to-all-start.3 = ((f32[16,2,32,256]{3,2,1,0:T(8,128)}), f32[16,2,32,256]{3,2,1,0:T(8,128)S(1)}, u32[]{:S(2)}, u32[]{:S(2)}) async-start(f32[16,2,32,256]{3,2,1,0:T(8,128)} %broadcast_in_dim.76), calls=%async_computation.3 | async-start | bytes 2097152 | tf_op jit(solution)/shard_map/all_to_all | solution.py:78
  99.8 10.6 %all-gather.7.cloned.1.call-done = f32[32,32,256]{2,1,0:T(8,128)} async-done(((f32[2,32,256]{2,1,0:T(8,128)}), f32[32,32,256]{2,1,0:T(8,128)}) %all-gather.7.cloned.1.call-update) | async-done | bytes 1048592 | tf_op jit(solution)/shard_map/all_gather | solution.py:67
  110.4 1.3 copy.55
  111.7 1.3 maximum_bitcast_fusion.2
  112.9 1.5 slice.321
  114.5 2.0 all-to-all-done.3
  117.2 101.4 %while.25 = (s32[]{:T(128)}, f32[256,256]{1,0:T(8,128)S(1)}, f32[2,256,256]{2,1,0:T(8,128)S(1)}, f32[2,256,256]{2,1,0:T(8,128)S(1)}, f32[2,256,256]{2,1,0:T(8,12...) while((s32[]{:T(128)}, f32[256,256]{1,0:T(8,128)S(1)}, ...), condition=%wide.region_4.7_spmd.clone, body=%wide.region_0.6_spmd.clone.sunk | while | flops 554959104 | bytes 6424720 | solution.py:104
  117.2 11.7 %cholesky.133 = f32[128,128]{1,0:T(8,128)S(1)} custom-call(f32[128,128]{1,0:T(8,128)S(1)} %slice.403), custom_call_target="Cholesky" | custom-call | tf_op jit(solution)/shard_map/while/body/eval_jaxpr/jit(cholesky)/cholesky | solution.py:12
  130.2 9.8 %custom-call.10 = f32[1,128,128]{1,2,0:T(8,128)S(1)} custom-call(f32[1,128,128]{2,1,0:T(8,128)S(1)} %get-tuple-element.352), custom_call_target="InvertDiagBlocksLowerTriangular" | custom-call | tf_op jit(solution)/shard_map/while/body/eval_jaxpr/jit(_solve_triangular)/triangular_solve | solution.py:13
  140.9 11.7 %cholesky.134 = f32[128,128]{1,0:T(8,128)S(1)} custom-call(f32[128,128]{1,0:T(8,128)S(1)} %convolution_subtract_fusion.6), custom_call_target="Cholesky" | custom-call | tf_op jit(solution)/shard_map/while/body/eval_jaxpr/jit(cholesky)/cholesky | solution.py:15
  153.8 9.8 %custom-call.11 = f32[1,128,128]{1,2,0:T(8,128)S(1)} custom-call(f32[1,128,128]{2,1,0:T(8,128)S(1)} %get-tuple-element.353), custom_call_target="InvertDiagBlocksLowerTriangular" | custom-call | tf_op jit(solution)/shard_map/while/body/eval_jaxpr/jit(_solve_triangular)/triangular_solve | solution.py:18
  167.8 11.7 %cholesky.133 = f32[128,128]{1,0:T(8,128)S(1)} custom-call(f32[128,128]{1,0:T(8,128)S(1)} %slice.403), custom_call_target="Cholesky" | custom-call | tf_op jit(solution)/shard_map/while/body/eval_jaxpr/jit(cholesky)/cholesky | solution.py:12
  180.8 9.8 %custom-call.10 = f32[1,128,128]{1,2,0:T(8,128)S(1)} custom-call(f32[1,128,128]{2,1,0:T(8,128)S(1)} %get-tuple-element.352), custom_call_target="InvertDiagBlocksLowerTriangular" | custom-call | tf_op jit(solution)/shard_map/while/body/eval_jaxpr/jit(_solve_triangular)/triangular_solve | solution.py:13
  191.5 11.7 %cholesky.134 = f32[128,128]{1,0:T(8,128)S(1)} custom-call(f32[128,128]{1,0:T(8,128)S(1)} %convolution_subtract_fusion.6), custom_call_target="Cholesky" | custom-call | tf_op jit(solution)/shard_map/while/body/eval_jaxpr/jit(cholesky)/cholesky | solution.py:15
  204.4 9.8 %custom-call.11 = f32[1,128,128]{1,2,0:T(8,128)S(1)} custom-call(f32[1,128,128]{2,1,0:T(8,128)S(1)} %get-tuple-element.353), custom_call_target="InvertDiagBlocksLowerTriangular" | custom-call | tf_op jit(solution)/shard_map/while/body/eval_jaxpr/jit(_solve_triangular)/triangular_solve | solution.py:18
  220.4 2.0 convolution_bitcast_fusion.2
  224.2 1.5 fusion.52
  226.5 1.4 convolution_subtract_fusion.3
  228.9 4.6 %convolution_subtract_fusion.2 = f32[3,256,3,256]{1,3,0,2:T(8,128)S(1)} fusion(f32[3,256,256]{1,2,0:T(8,128)S(1)} %fusion.33, f32[3,256,256]{1,2,0:T(8,128)S(1)} %fusion.38, f32[3,256,256]{2,1,0:T(8,128)S(1)} %convolution_bitcast_fusion, f32[3,256,256]{2,1,0:T(8,128)S(1)} %convolution_bitcast_fusion.2, f32[3,1,256,3,1,256]{2,5,0,3,4,1:T(8,128)S(1)} %copy-done.1), kind=kOutput, calls=%fused_computation.38 | convolution fusion | flops 3625254912 | bytes 7864320 | tf_op jit(solution)/shard_map/aik,bkj->aibj/dot_general | solution.py:122
  234.4 4.3 %copy.63 = f32[3,1,256,3,1,256]{5,4,3,2,1,0:T(1,128)} copy(f32[3,1,256,3,1,256]{2,5,0,3,4,1:T(8,128)S(1)} %fusion.27) | data formatting | bytes 4718592 | tf_op jit(solution)/shard_map/scatter | solution.py:132
  (94 shorter events, 24.0 us)
Async XLA Ops:
  7.4 1.1 slice-start
  41.4 0.9 copy-start.7
  43.2 20.2 %all-to-all-start.1 = ((f32[16,2,16,256]{3,2,1,0:T(8,128)}), f32[16,2,16,256]{3,2,1,0:T(8,128)S(1)}, u32[]{:S(2)}, u32[]{:S(2)}) async-start(f32[16,2,16,256]{3,2,1,0:T(8,128)} %broadcast_in_dim.75), calls=%async_computation.1 | async-start | bytes 1048576 | tf_op jit(solution)/shard_map/all_to_all | solution.py:60
  52.1 3.4 %copy-start = (f32[3,1,256,3,1,256]{2,5,0,3,4,1:T(8,128)}, f32[3,1,256,3,1,256]{2,5,0,3,4,1:T(8,128)S(1)}, u32[]{:S(2)}) copy-start(f32[3,1,256,3,1,256]{2,5,0,3,4,1:T(8,128)S(1)} %copy.49) | copy-start | bytes 7077892
  55.5 8.0 %copy-start.3 = (f32[3,256,1,256]{3,1,0,2:T(8,128)S(1)}, f32[3,256,1,256]{3,1,0,2:T(8,128)}, u32[]{:S(2)}) copy-start(f32[3,256,1,256]{3,1,0,2:T(8,128)} %copy.50) | copy-start | bytes 2359300
  64.7 29.8 %all-to-all-start.2 = ((f32[16,80,256]{2,1,0:T(8,128)}), f32[16,80,256]{2,1,0:T(8,128)S(1)}, u32[]{:S(2)}, u32[]{:S(2)}) async-start(f32[16,80,256]{2,1,0:T(8,128)} %pad_maximum_fusion), calls=%async_computation.2 | async-start | bytes 2621440 | tf_op jit(solution)/shard_map/all_to_all | solution.py:76
  71.4 38.9 %all-gather.7.cloned.1.call-start = ((), (), s32[]{:S(2)}) async-start(), calls=%async_computation.5 | async-start | bytes 1114112 | tf_op jit(solution)/shard_map/all_gather | solution.py:67
  94.5 1.4 copy-start.4
  95.9 20.5 %all-to-all-start.3 = ((f32[16,2,32,256]{3,2,1,0:T(8,128)}), f32[16,2,32,256]{3,2,1,0:T(8,128)S(1)}, u32[]{:S(2)}, u32[]{:S(2)}) async-start(f32[16,2,32,256]{3,2,1,0:T(8,128)} %broadcast_in_dim.76), calls=%async_computation.3 | async-start | bytes 2097152 | tf_op jit(solution)/shard_map/all_to_all | solution.py:78
  99.6 124.5 %all-gather.5.cloned.1.call-start = ((), (), s32[]{:S(2)}) async-start(), calls=%async_computation.4 | async-start | bytes 1671168 | tf_op jit(solution)/shard_map/all_gather | solution.py:86
  116.6 0.7 copy-start.8
  218.7 3.7 %copy-start.2 = (f32[2,256,3,256]{3,1,2,0:T(8,128)S(1)}, f32[2,256,3,256]{3,1,2,0:T(8,128)}, u32[]{:S(2)}) copy-start(f32[2,256,3,256]{3,1,2,0:T(8,128)} %maximum_bitcast_fusion.2) | copy-start | bytes 4718596
  226.5 2.3 copy-start.1
  228.8 4.7 %copy-start.5 = (f32[256,256]{0,1:T(8,128)S(1)}, f32[256,256]{0,1:T(8,128)}, u32[]{:S(2)}) copy-start(f32[256,256]{0,1:T(8,128)} %copy.60) | copy-start | bytes 786436
  228.9 4.7 %copy-start.6 = (f32[256,256]{0,1:T(8,128)S(1)}, f32[256,256]{0,1:T(8,128)}, u32[]{:S(2)}) copy-start(f32[256,256]{0,1:T(8,128)} %copy.61) | copy-start | bytes 786436
Sparse Core Ops, SparseCore 0:
  74.1 36.1 all-gather.6
Sparse Core Ops, SparseCore 1:
  114.6 45.8 all-gather.4
where the time goes:
time: 247 us; the launch traced here: 246 us
  other arithmetic  98.1 us (40%)
  waiting for transfers between devices  42 us (17%)
  blocking collectives  32.7 us (13%)
  local copies, waits for them, and re-layouts  26.7 us (11%)
  matrix products  16.9 us (7%)
  between operations  15.2 us (6%)
  starting transfers between devices  14 us (6%)
    all_to_all x1, blocking collectives, on_device(): lax.all_to_all(jnp.concatenate([top_first, top_rest], axis=1), 'prow', 0,...  32.7 us
    another operation x6, other arithmetic, chol_and_inverse(): jnp.linalg.cholesky(block[h:, h:] - jnp.dot(lb, lb.T, precision=HIGH), sy...  24.7 us
    another operation x6, other arithmetic, chol_and_inverse(): la = jnp.linalg.cholesky(block[:h, :h], symmetrize_input=False)  24.7 us
    all_to_all x1, waiting for transfers between devices, on_device(): mine = lax.all_to_all(pieces, 'pcol', 0, 0, tiled=False)  21.5 us
    another operation x4, other arithmetic, chol_and_inverse(): wc = jax.scipy.linalg.solve_triangular(lc, small, lower=True)  20.8 us
    another operation x4, other arithmetic, chol_and_inverse(): wa = jax.scipy.linalg.solve_triangular(la, small, lower=True)  20.8 us
    all_gather x1, waiting for transfers between devices, on_device(): lax.all_gather(top_kept[:, split:], 'prow', axis=0, tiled=False)  10.6 us
    all_to_all x1, waiting for transfers between devices, on_device(): lax.all_to_all(jnp.broadcast_to(top_kept[None, :, :split], (rows, 2, spli...  7.9 us
  transfers between devices with their start and end apart: 5, of which 4 were waited for; matrix products, arithmetic and copies ran while one was open for 50% of the time, Pallas kernels for 0%

commit v1 on v0

--- a/solution.py
+++ b/solution.py
@@ -91,8 +91,13 @@
     def factor_step(k, carry):
         block, lowers, inverses, panels = carry
         lower, inverse = chol_and_inverse(block, eye)
-        panel = jnp.dot(m10, inverse.T, precision=HIGH)
-        nxt = m11 - jnp.dot(panel, panel.T, precision=HIGH)
+        def next_block(w):
+            panel = jnp.dot(m10, w.T, precision=HIGH)
+            return m11 - jnp.dot(panel, panel.T, precision=HIGH), panel
+
+        nxt, panel = lax.cond(
+            k == 0, next_block, lambda w: (block, jnp.zeros_like(block)), inverse
+        )
         return (
             nxt,
             lowers.at[k].set(lower),

time: 247 us -> 277 us (1.12)
  local copies, waits for them, and re-layouts: 26.7 us -> 37.9 us
  matrix products: 16.9 us -> 27 us
  other arithmetic: 98.1 us -> 106 us
    scatter x2, other arithmetic: 1.22 us -> 4.79 us  [factor_step(): panels.at[k].set(panel)]
    scatter x2, other arithmetic: 1.31 us -> 4.68 us  [factor_step(): lowers.at[k].set(lower)]
    broadcast_in_dim x2, local copies, waits for them, and re-layouts: 0.86 us -> 3.7 us  [on_device(): col0 = jnp.where(rk == 0, l0[None], r0)]
    unnamed x21 -> x23, local copies, waits for them, and re-layouts: 7.34 us -> 8.2 us
  transfers between devices with their start and end apart: 5 -> 5, of which waited for: 4 -> 4; matrix products, arithmetic and copies ran while one was open for 50% -> 55% of each run, Pallas kernels for 0% -> 0%
where the time goes in v1:
time: 277 us; the launch traced here: 275 us
  other arithmetic  106 us (38%)
  waiting for transfers between devices  41.6 us (15%)
  local copies, waits for them, and re-layouts  37.9 us (14%)
  blocking collectives  32.7 us (12%)
  matrix products  27 us (10%)
  between operations  15.1 us (5%)
  starting transfers between devices  14.7 us (5%)
    all_to_all x1, blocking collectives, on_device(): lax.all_to_all(jnp.concatenate([top_first, top_rest], axis=1), 'prow', 0,...  32.7 us
    another operation x6, other arithmetic, chol_and_inverse(): jnp.linalg.cholesky(block[h:, h:] - jnp.dot(lb, lb.T, precision=HIGH), sy...  24.8 us
    another operation x6, other arithmetic, chol_and_inverse(): la = jnp.linalg.cholesky(block[:h, :h], symmetrize_input=False)  24.8 us
    all_to_all x1, waiting for transfers between devices, on_device(): mine = lax.all_to_all(pieces, 'pcol', 0, 0, tiled=False)  21.6 us
    another operation x4, other arithmetic, chol_and_inverse(): wa = jax.scipy.linalg.solve_triangular(la, small, lower=True)  20.9 us
    another operation x4, other arithmetic, chol_and_inverse(): wc = jax.scipy.linalg.solve_triangular(lc, small, lower=True)  20.9 us
    all_gather x1, waiting for transfers between devices, on_device(): lax.all_gather(top_kept[:, split:], 'prow', axis=0, tiled=False)  8.56 us
    unnamed x23, local copies, waits for them, and re-layouts  8.2 us
  transfers between devices with their start and end apart: 5, of which 4 were waited for; matrix products, arithmetic and copies ran while one was open for 55% of the time, Pallas kernels for 0%

profile of v1, /device:TPU:1, one launch (start us, length us, event | category | flops | bytes accessed | tf_op | source)
XLA Modules:
  0.0 275.3 jit_solution(10334243226415800323)
XLA Ops:
  8.7 32.7 %all_to_all.20 = f32[16,48,256]{2,1,0:T(8,128)S(1)} all-to-all(f32[16,48,256]{2,1,0:T(8,128)S(1)} %pad_maximum_fusion.1), channel_id=1, replica_groups=mesh['prow'=16,'pcol'=16] {'prow'}, dimensions={0} | all-to-all | bytes 1572864 | tf_op jit(solution)/shard_map/all_to_all | solution.py:56
  42.4 3.5 %all-to-all-start.1 = ((f32[16,2,16,256]{3,2,1,0:T(8,128)}), f32[16,2,16,256]{3,2,1,0:T(8,128)S(1)}, u32[]{:S(2)}, u32[]{:S(2)}) async-start(f32[16,2,16,256]{3,2,1,0:T(8,128)} %broadcast_in_dim.75), calls=%async_computation.1 | async-start | bytes 1048576 | tf_op jit(solution)/shard_map/all_to_all | solution.py:60
  45.9 5.5 %copy.45 = f32[3,1,256,3,1,256]{2,5,0,3,4,1:T(8,128)S(1)} copy(f32[3,1,256,3,1,256]{5,4,3,2,1,0:T(1,128)} %param.18) | data formatting | bytes 4718592 | tf_op args[0]
  52.3 2.3 copy.46
  54.6 8.0 %all-to-all-done.1 = f32[16,2,16,256]{3,2,1,0:T(8,128)S(1)} async-done(((f32[16,2,16,256]{3,2,1,0:T(8,128)}), f32[16,2,16,256]{3,2,1,0:T(8,128)S(1)}, u32[]{:S(2)}, u32[]{:S(2)}) %all-to-all-start.1) | async-done | bytes 524320 | tf_op jit(solution)/shard_map/all_to_all | solution.py:60
  64.9 6.8 %all-to-all-start.2 = ((f32[16,80,256]{2,1,0:T(8,128)}), f32[16,80,256]{2,1,0:T(8,128)}, u32[]{:S(2)}, u32[]{:S(2)}) async-start(f32[16,80,256]{2,1,0:T(8,128)} %pad_maximum_fusion), calls=%async_computation.2 | async-start | bytes 2621440 | tf_op jit(solution)/shard_map/all_to_all | solution.py:76
  73.3 21.6 %all-to-all-done.2 = f32[16,80,256]{2,1,0:T(8,128)} async-done(((f32[16,80,256]{2,1,0:T(8,128)}), f32[16,80,256]{2,1,0:T(8,128)}, u32[]{:S(2)}, u32[]{:S(2)}) %all-to-all-start.2) | async-done | bytes 1310752 | tf_op jit(solution)/shard_map/all_to_all | solution.py:76
  96.8 4.3 %all-to-all-start.3 = ((f32[16,2,32,256]{3,2,1,0:T(8,128)}), f32[16,2,32,256]{3,2,1,0:T(8,128)}, u32[]{:S(2)}, u32[]{:S(2)}) async-start(f32[16,2,32,256]{3,2,1,0:T(8,128)} %broadcast_in_dim.76), calls=%async_computation.3 | async-start | bytes 2097152 | tf_op jit(solution)/shard_map/all_to_all | solution.py:78
  102.0 8.6 %all-gather.7.cloned.1.call-done = f32[32,32,256]{2,1,0:T(8,128)} async-done(((f32[2,32,256]{2,1,0:T(8,128)}), f32[32,32,256]{2,1,0:T(8,128)}) %all-gather.7.cloned.1.call-update) | async-done | bytes 1048592 | tf_op jit(solution)/shard_map/all_gather | solution.py:67
  114.7 3.3 %all-to-all-done.3 = f32[16,2,32,256]{3,2,1,0:T(8,128)} async-done(((f32[16,2,32,256]{3,2,1,0:T(8,128)}), f32[16,2,32,256]{3,2,1,0:T(8,128)}, u32[]{:S(2)}, u32[]{:S(2)}) %all-to-all-start.3) | async-done | bytes 1048608 | tf_op jit(solution)/shard_map/all_to_all | solution.py:78
  122.1 119.7 %while.28 = (s32[]{:T(128)}, f32[256,256]{1,0:T(8,128)}, f32[2,256,256]{2,1,0:T(8,128)}, f32[2,256,256]{2,1,0:T(8,128)S(1)}, f32[2,256,256]{2,1,0:T(8,128)}, /*i...) while((s32[]{:T(128)}, f32[256,256]{1,0:T(8,128)}, ...), condition=%wide.region_6.9_spmd.clone, body=%wide.region_0.8_spmd.clone.sunk | while | flops 554893568 | bytes 6426820 | solution.py:109
  122.9 11.7 %cholesky.133 = f32[128,128]{1,0:T(8,128)S(1)} custom-call(f32[128,128]{1,0:T(8,128)S(1)} %slice.403), custom_call_target="Cholesky" | custom-call | tf_op jit(solution)/shard_map/while/body/eval_jaxpr/jit(cholesky)/cholesky | solution.py:12
  135.9 9.8 %custom-call.10 = f32[1,128,128]{1,2,0:T(8,128)S(1)} custom-call(f32[1,128,128]{2,1,0:T(8,128)S(1)} %get-tuple-element.371), custom_call_target="InvertDiagBlocksLowerTriangular" | custom-call | tf_op jit(solution)/shard_map/while/body/eval_jaxpr/jit(_solve_triangular)/triangular_solve | solution.py:13
  149.1 11.7 %cholesky.134 = f32[128,128]{1,0:T(8,128)S(1)} custom-call(f32[128,128]{1,0:T(8,128)S(1)} %convolution_subtract_fusion.5), custom_call_target="Cholesky" | custom-call | tf_op jit(solution)/shard_map/while/body/eval_jaxpr/jit(cholesky)/cholesky | solution.py:15
  162.2 9.8 %custom-call.11 = f32[1,128,128]{1,2,0:T(8,128)S(1)} custom-call(f32[1,128,128]{2,1,0:T(8,128)S(1)} %get-tuple-element.372), custom_call_target="InvertDiagBlocksLowerTriangular" | custom-call | tf_op jit(solution)/shard_map/while/body/eval_jaxpr/jit(_solve_triangular)/triangular_solve | solution.py:18
  174.6 2.3 fusion.98
  177.0 4.3 %conditional.3 = (f32[256,256]{1,0:T(8,128)}, f32[1,256,256]{2,1,0:T(8,128)}) conditional(s32[]{:T(128)} %convert_element_type.16, f32[256,256]{1,0:T(8,128)} %get-tuple-element.396, (f32[256,256]{1,0:T(8,128)}, f32[256,256]{1,0:T(8,128)S(1)}, f32[256,256]{1,0:T(8,128)}) %tuple.96), branch_computations={%region_3.5_spmd, %region_4.6_spmd} | conditional | flops 402718720 | bytes 1572880 | solution.py:98
  177.0 2.1 fusion.47
  179.1 2.2 convolution_subtract_fusion
  181.3 2.4 select_dynamic-update-slice_fusion.2
  184.5 11.7 %cholesky.133 = f32[128,128]{1,0:T(8,128)S(1)} custom-call(f32[128,128]{1,0:T(8,128)S(1)} %slice.403), custom_call_target="Cholesky" | custom-call | tf_op jit(solution)/shard_map/while/body/eval_jaxpr/jit(cholesky)/cholesky | solution.py:12
  197.6 9.8 %custom-call.10 = f32[1,128,128]{1,2,0:T(8,128)S(1)} custom-call(f32[1,128,128]{2,1,0:T(8,128)S(1)} %get-tuple-element.371), custom_call_target="InvertDiagBlocksLowerTriangular" | custom-call | tf_op jit(solution)/shard_map/while/body/eval_jaxpr/jit(_solve_triangular)/triangular_solve | solution.py:13
  210.7 11.7 %cholesky.134 = f32[128,128]{1,0:T(8,128)S(1)} custom-call(f32[128,128]{1,0:T(8,128)S(1)} %convolution_subtract_fusion.5), custom_call_target="Cholesky" | custom-call | tf_op jit(solution)/shard_map/while/body/eval_jaxpr/jit(cholesky)/cholesky | solution.py:15
  223.8 9.8 %custom-call.11 = f32[1,128,128]{1,2,0:T(8,128)S(1)} custom-call(f32[1,128,128]{2,1,0:T(8,128)S(1)} %get-tuple-element.372), custom_call_target="InvertDiagBlocksLowerTriangular" | custom-call | tf_op jit(solution)/shard_map/while/body/eval_jaxpr/jit(_solve_triangular)/triangular_solve | solution.py:18
  236.2 2.3 fusion.98
  239.3 2.4 select_dynamic-update-slice_fusion.2
  241.7 1.9 slice_bitcast_fusion.9
  243.6 1.8 copy.56
  245.4 1.8 copy.57
  247.2 2.1 convolution_bitcast_fusion.2
  258.0 4.7 %convolution_subtract_fusion.2 = f32[3,256,3,256]{1,3,0,2:T(8,128)S(1)} fusion(f32[3,256,256]{1,2,0:T(8,128)S(1)} %fusion.26, f32[3,256,256]{1,2,0:T(8,128)S(1)} %fusion.31, f32[3,256,256]{2,1,0:T(8,128)S(1)} %copy-done.5, f32[3,256,256]{2,1,0:T(8,128)S(1)} %copy-done.2, f32[3,1,256,3,1,256]{2,5,0,3,4,1:T(8,128)S(1)} %copy.45), kind=kOutput, calls=%fused_computation.31 | convolution fusion | flops 3625254912 | bytes 7864320 | tf_op jit(solution)/shard_map/aik,bkj->aibj/dot_general | solution.py:127
  263.6 4.3 %copy.59 = f32[3,1,256,3,1,256]{5,4,3,2,1,0:T(1,128)} copy(f32[3,1,256,3,1,256]{2,5,0,3,4,1:T(8,128)S(1)} %fusion.20) | data formatting | bytes 4718592 | tf_op jit(solution)/shard_map/scatter | solution.py:137
  (97 shorter events, 47.7 us)
Async XLA Ops:
  7.4 1.1 slice-start
  41.4 4.5 %copy-start.8 = (f32[16,48,256]{2,1,0:T(8,128)}, f32[16,48,256]{2,1,0:T(8,128)S(1)}, u32[]{:S(2)}) copy-start(f32[16,48,256]{2,1,0:T(8,128)S(1)} %all_to_all.20) | copy-start | bytes 2359300
  42.4 20.2 %all-to-all-start.1 = ((f32[16,2,16,256]{3,2,1,0:T(8,128)}), f32[16,2,16,256]{3,2,1,0:T(8,128)S(1)}, u32[]{:S(2)}, u32[]{:S(2)}) async-start(f32[16,2,16,256]{3,2,1,0:T(8,128)} %broadcast_in_dim.75), calls=%async_computation.1 | async-start | bytes 1048576 | tf_op jit(solution)/shard_map/all_to_all | solution.py:60
  62.7 1.1 copy-start.4
  64.9 29.9 %all-to-all-start.2 = ((f32[16,80,256]{2,1,0:T(8,128)}), f32[16,80,256]{2,1,0:T(8,128)}, u32[]{:S(2)}, u32[]{:S(2)}) async-start(f32[16,80,256]{2,1,0:T(8,128)} %pad_maximum_fusion), calls=%async_computation.2 | async-start | bytes 2621440 | tf_op jit(solution)/shard_map/all_to_all | solution.py:76
  71.7 38.9 %all-gather.7.cloned.1.call-start = ((), (), s32[]{:S(2)}) async-start(), calls=%async_computation.5 | async-start | bytes 1114112 | tf_op jit(solution)/shard_map/all_gather | solution.py:67
  96.8 21.3 %all-to-all-start.3 = ((f32[16,2,32,256]{3,2,1,0:T(8,128)}), f32[16,2,32,256]{3,2,1,0:T(8,128)}, u32[]{:S(2)}, u32[]{:S(2)}) async-start(f32[16,2,32,256]{3,2,1,0:T(8,128)} %broadcast_in_dim.76), calls=%async_computation.3 | async-start | bytes 2097152 | tf_op jit(solution)/shard_map/all_to_all | solution.py:78
  101.2 151.7 %all-gather.5.cloned.1.call-start = ((), (), s32[]{:S(2)}) async-start(), calls=%async_computation.4 | async-start | bytes 1671168 | tf_op jit(solution)/shard_map/all_gather | solution.py:86
  119.4 2.7 copy-start.9
  243.6 6.6 %copy-start = (f32[2,256,256]{2,1,0:T(8,128)S(1)}, f32[2,256,256]{2,1,0:T(8,128)}, u32[]{:S(2)}) copy-start(f32[2,256,256]{2,1,0:T(8,128)} %get-tuple-element.257) | copy-start | bytes 1572868
  247.2 3.0 %copy-start.3 = (f32[2,256,3,256]{3,1,2,0:T(8,128)S(1)}, f32[2,256,3,256]{3,1,2,0:T(8,128)}, u32[]{:S(2)}) copy-start(f32[2,256,3,256]{3,1,2,0:T(8,128)} %maximum_bitcast_fusion.2) | copy-start | bytes 4718596
  249.3 0.9 copy-start.1
  256.6 1.1 copy-start.2
  256.6 1.4 copy-start.5
  258.0 4.8 %copy-start.6 = (f32[256,256]{0,1:T(8,128)S(1)}, f32[256,256]{0,1:T(8,128)}, u32[]{:S(2)}) copy-start(f32[256,256]{0,1:T(8,128)} %copy.56) | copy-start | bytes 786436
  258.0 4.8 %copy-start.7 = (f32[256,256]{0,1:T(8,128)S(1)}, f32[256,256]{0,1:T(8,128)}, u32[]{:S(2)}) copy-start(f32[256,256]{0,1:T(8,128)} %copy.57) | copy-start | bytes 786436
Sparse Core Ops, SparseCore 0:
  74.4 36.1 all-gather.6
Sparse Core Ops, SparseCore 1:
  114.8 46.7 all-gather.4

commit v2 on v0

--- a/solution.py
+++ b/solution.py
@@ -50,8 +50,10 @@
     eye = jnp.eye(blk, dtype=jnp.float32)
 
     top = work[0]
-    top_first = top[:, 0, :].reshape(rows, -1, blk)
-    top_rest = jnp.swapaxes(top[:, 1:, :], 0, 1).reshape(rows, -1, blk)
+    top_rows = jnp.swapaxes(top, 0, 1).reshape(-1, blk)
+    half = top_rows.shape[0] // 2
+    top_first = top_rows[:half].reshape(rows, -1, blk)
+    top_rest = top_rows[half:].reshape(rows, -1, blk)
     split = top_first.shape[1]
     top_mine = lax.all_to_all(
         jnp.concatenate([top_first, top_rest], axis=1), "prow", 0, 0, tiled=False
@@ -61,12 +63,13 @@
         jnp.broadcast_to(top_kept[None, :, :split], (rows, 2, split, blk)),
         "prow", 0, 0, tiled=False,
     )
-    y_first = jnp.swapaxes(top_spread, 0, 1).reshape(2, blk, blk)
-    y0c = y_first[0]
-    y1c = y_first[1]
+    y_first = jnp.swapaxes(top_spread, 0, 1).reshape(2, -1, blk)
+    y0c = y_first[0, :blk]
+    y1c = y_first[1, :blk]
     top_gathered = lax.all_gather(top_kept[:, split:], "prow", axis=0, tiled=False)
-    y_rest = jnp.swapaxes(top_gathered, 0, 1).reshape(2, lbc - 1, blk, blk)
-    ytop = jnp.concatenate([y_first[:, None], y_rest], axis=1).transpose(0, 2, 1, 3)
+    y_rest = jnp.swapaxes(top_gathered, 0, 1).reshape(2, -1, blk)
+    ytop = jnp.concatenate([y_first, y_rest], axis=1).reshape(2, lbc, blk, blk)
+    ytop = ytop.transpose(0, 2, 1, 3)
 
     extra = jnp.where(pcol == 0, jnp.stack([y0c, y1c]), jnp.stack([y1c, jnp.zeros_like(y1c)]))
     panel = work[:, :, 0, :].reshape(cols, -1, blk)

time: 247 us -> 251 us (1.016)
  blocking collectives: 32.7 us -> 75.7 us
  waiting for transfers between devices: 42 us -> 13.2 us
  starting transfers between devices: 14 us -> 7.2 us
    all_to_all x0 -> x1, blocking collectives: none -> 26.1 us  [on_device(): mine = lax.all_to_all(pieces, 'pcol', 0, 0, tiled=False)]
    all_to_all x1 -> x0, waiting for transfers between devices: 21.5 us -> none  [on_device(): mine = lax.all_to_all(pieces, 'pcol', 0, 0, tiled=False)]
    all_gather x0 -> x1, blocking collectives: none -> 16.9 us  [on_device(): lax.all_gather(top_kept[:, split:], 'prow', axis=0, tiled=False)]
    all_gather x1 -> x0, waiting for transfers between devices: 10.6 us -> none  [on_device(): lax.all_gather(top_kept[:, split:], 'prow', axis=0, tiled=False)]
    all_to_all x1 -> x0, starting transfers between devices: 6.75 us -> none  [on_device(): mine = lax.all_to_all(pieces, 'pcol', 0, 0, tiled=False)]
    all_to_all x1, waiting for transfers between devices: 7.9 us -> 13.2 us  [on_device(): lax.all_to_all(jnp.broadcast_to(top_kept[None, :, :split], (rows, 2, spli...]
    unnamed x21 -> x19, local copies, waits for them, and re-layouts: 7.34 us -> 8.3 us
  transfers between devices with their start and end apart: 5 -> 3, of which waited for: 4 -> 1; matrix products, arithmetic and copies ran while one was open for 50% -> 48% of each run, Pallas kernels for 0% -> 0%
where the time goes in v2:
time: 251 us; the launch traced here: 250 us
  other arithmetic  97.9 us (39%)
  blocking collectives  75.7 us (30%)
  local copies, waits for them, and re-layouts  25 us (10%)
  matrix products  16.9 us (7%)
  between operations  13.8 us (5%)
  waiting for transfers between devices  13.2 us (5%)
  starting transfers between devices  7.2 us (3%)
    all_to_all x1, blocking collectives, on_device(): lax.all_to_all(jnp.concatenate([top_first, top_rest], axis=1), 'prow', 0,...  32.7 us
    all_to_all x1, blocking collectives, on_device(): mine = lax.all_to_all(pieces, 'pcol', 0, 0, tiled=False)  26.1 us
    another operation x6, other arithmetic, chol_and_inverse(): jnp.linalg.cholesky(block[h:, h:] - jnp.dot(lb, lb.T, precision=HIGH), sy...  24.8 us
    another operation x6, other arithmetic, chol_and_inverse(): la = jnp.linalg.cholesky(block[:h, :h], symmetrize_input=False)  24.8 us
    another operation x4, other arithmetic, chol_and_inverse(): wa = jax.scipy.linalg.solve_triangular(la, small, lower=True)  20.9 us
    another operation x4, other arithmetic, chol_and_inverse(): wc = jax.scipy.linalg.solve_triangular(lc, small, lower=True)  20.9 us
    all_gather x1, blocking collectives, on_device(): lax.all_gather(top_kept[:, split:], 'prow', axis=0, tiled=False)  16.9 us
    all_to_all x1, waiting for transfers between devices, on_device(): lax.all_to_all(jnp.broadcast_to(top_kept[None, :, :split], (rows, 2, spli...  13.2 us
  transfers between devices with their start and end apart: 3, of which 1 were waited for; matrix products, arithmetic and copies ran while one was open for 48% of the time, Pallas kernels for 0%

profile of v2, /device:TPU:1, one launch (start us, length us, event | category | flops | bytes accessed | tf_op | source)
XLA Modules:
  0.0 250.1 jit_solution(1200772260638440203)
XLA Ops:
  6.5 1.1 slice-done
  7.9 32.7 %all_to_all.20 = f32[16,48,256]{2,1,0:T(8,128)S(1)} all-to-all(f32[16,48,256]{2,1,0:T(8,128)S(1)} %pad_maximum_fusion.2), channel_id=1, replica_groups=mesh['prow'=16,'pcol'=16] {'prow'}, dimensions={0} | all-to-all | bytes 1572864 | tf_op jit(solution)/shard_map/all_to_all | solution.py:58
  40.6 1.0 broadcast_in_dim.75
  41.6 3.5 %all-to-all-start.1 = ((f32[16,2,24,256]{3,2,1,0:T(8,128)}), f32[16,2,24,256]{3,2,1,0:T(8,128)S(1)}, u32[]{:S(2)}, u32[]{:S(2)}) async-start(f32[16,2,24,256]{3,2,1,0:T(8,128)} %broadcast_in_dim.75), calls=%async_computation.1 | async-start | bytes 1572864 | tf_op jit(solution)/shard_map/all_to_all | solution.py:62
  45.1 5.5 %copy.65 = f32[3,1,256,3,1,256]{2,5,0,3,4,1:T(8,128)S(1)} copy(f32[3,1,256,3,1,256]{5,4,3,2,1,0:T(1,128)} %param.16) | data formatting | bytes 4718592 | tf_op args[0]
  50.6 1.0 slice.305
  51.6 2.4 copy.66
  54.0 13.2 %all-to-all-done.1 = f32[16,2,24,256]{3,2,1,0:T(8,128)S(1)} async-done(((f32[16,2,24,256]{3,2,1,0:T(8,128)}), f32[16,2,24,256]{3,2,1,0:T(8,128)S(1)}, u32[]{:S(2)}, u32[]{:S(2)}) %all-to-all-start.1) | async-done | bytes 786464 | tf_op jit(solution)/shard_map/all_to_all | solution.py:62
  67.3 1.0 copy-done.3
  68.3 26.1 %all_to_all.21 = f32[16,80,256]{2,1,0:T(8,128)S(1)} all-to-all(f32[16,80,256]{2,1,0:T(8,128)S(1)} %pad_maximum_fusion.1), channel_id=1, replica_groups=mesh['prow'=16,'pcol'=16] {'pcol'}, dimensions={0} | all-to-all | bytes 2621440 | tf_op jit(solution)/shard_map/all_to_all | solution.py:79
  94.4 1.1 copy-done.4
  95.5 1.1 broadcast_in_dim.76
  96.6 3.7 %all-to-all-start.3 = ((f32[16,2,32,256]{3,2,1,0:T(8,128)}), f32[16,2,32,256]{3,2,1,0:T(8,128)S(1)}, u32[]{:S(2)}, u32[]{:S(2)}) async-start(f32[16,2,32,256]{3,2,1,0:T(8,128)} %broadcast_in_dim.76), calls=%async_computation.3 | async-start | bytes 2097152 | tf_op jit(solution)/shard_map/all_to_all | solution.py:81
  100.4 16.9 %all-gather.1 = f32[32,24,256]{2,1,0:T(8,128)S(1)} all-gather(f32[2,24,256]{2,1,0:T(8,128)S(1)} %get-tuple-element.291), channel_id=3, replica_groups=mesh['prow'=16,'pcol'=16] {'prow'}, dimensions={0}, use_global_device_ids=true | all-gather | bytes 835584 | tf_op jit(solution)/shard_map/all_gather | solution.py:69
  117.4 1.3 pad_maximum_fusion
  118.6 1.5 slice.310
  121.0 102.3 %while.25 = (s32[]{:T(128)}, f32[256,256]{1,0:T(8,128)S(1)}, f32[2,256,256]{2,1,0:T(8,128)S(1)}, f32[2,256,256]{2,1,0:T(8,128)S(1)}, f32[2,256,256]{2,1,0:T(8,12...) while((s32[]{:T(128)}, f32[256,256]{1,0:T(8,128)S(1)}, ...), condition=%wide.region_4.7_spmd.clone, body=%wide.region_0.6_spmd.clone.sunk | while | flops 554959104 | bytes 6424720 | solution.py:107
  121.0 11.7 %cholesky.133 = f32[128,128]{1,0:T(8,128)S(1)} custom-call(f32[128,128]{1,0:T(8,128)S(1)} %slice.394), custom_call_target="Cholesky" | custom-call | tf_op jit(solution)/shard_map/while/body/eval_jaxpr/jit(cholesky)/cholesky | solution.py:12
  134.0 9.8 %custom-call.10 = f32[1,128,128]{1,2,0:T(8,128)S(1)} custom-call(f32[1,128,128]{2,1,0:T(8,128)S(1)} %get-tuple-element.354), custom_call_target="InvertDiagBlocksLowerTriangular" | custom-call | tf_op jit(solution)/shard_map/while/body/eval_jaxpr/jit(_solve_triangular)/triangular_solve | solution.py:13
  144.7 11.7 %cholesky.134 = f32[128,128]{1,0:T(8,128)S(1)} custom-call(f32[128,128]{1,0:T(8,128)S(1)} %convolution_subtract_fusion.6), custom_call_target="Cholesky" | custom-call | tf_op jit(solution)/shard_map/while/body/eval_jaxpr/jit(cholesky)/cholesky | solution.py:15
  157.8 9.8 %custom-call.11 = f32[1,128,128]{1,2,0:T(8,128)S(1)} custom-call(f32[1,128,128]{2,1,0:T(8,128)S(1)} %get-tuple-element.355), custom_call_target="InvertDiagBlocksLowerTriangular" | custom-call | tf_op jit(solution)/shard_map/while/body/eval_jaxpr/jit(_solve_triangular)/triangular_solve | solution.py:18
  172.0 11.7 %cholesky.133 = f32[128,128]{1,0:T(8,128)S(1)} custom-call(f32[128,128]{1,0:T(8,128)S(1)} %slice.394), custom_call_target="Cholesky" | custom-call | tf_op jit(solution)/shard_map/while/body/eval_jaxpr/jit(cholesky)/cholesky | solution.py:12
  185.1 9.8 %custom-call.10 = f32[1,128,128]{1,2,0:T(8,128)S(1)} custom-call(f32[1,128,128]{2,1,0:T(8,128)S(1)} %get-tuple-element.354), custom_call_target="InvertDiagBlocksLowerTriangular" | custom-call | tf_op jit(solution)/shard_map/while/body/eval_jaxpr/jit(_solve_triangular)/triangular_solve | solution.py:13
  195.7 11.7 %cholesky.134 = f32[128,128]{1,0:T(8,128)S(1)} custom-call(f32[128,128]{1,0:T(8,128)S(1)} %convolution_subtract_fusion.6), custom_call_target="Cholesky" | custom-call | tf_op jit(solution)/shard_map/while/body/eval_jaxpr/jit(cholesky)/cholesky | solution.py:15
  208.8 9.8 %custom-call.11 = f32[1,128,128]{1,2,0:T(8,128)S(1)} custom-call(f32[1,128,128]{2,1,0:T(8,128)S(1)} %get-tuple-element.355), custom_call_target="InvertDiagBlocksLowerTriangular" | custom-call | tf_op jit(solution)/shard_map/while/body/eval_jaxpr/jit(_solve_triangular)/triangular_solve | solution.py:18
  225.0 2.0 convolution_bitcast_fusion.2
  227.0 0.9 fusion.24
  227.9 0.9 convolution_bitcast_fusion
  228.7 1.5 fusion.52
  231.1 1.4 convolution_subtract_fusion.3
  233.5 4.6 %convolution_subtract_fusion.2 = f32[3,256,3,256]{1,3,0,2:T(8,128)S(1)} fusion(f32[3,256,256]{1,2,0:T(8,128)S(1)} %fusion.33, f32[3,256,256]{1,2,0:T(8,128)S(1)} %fusion.38, f32[3,256,256]{2,1,0:T(8,128)S(1)} %convolution_bitcast_fusion, f32[3,256,256]{2,1,0:T(8,128)S(1)} %convolution_bitcast_fusion.2, f32[3,1,256,3,1,256]{2,5,0,3,4,1:T(8,128)S(1)} %copy-done.1), kind=kOutput, calls=%fused_computation.38 | convolution fusion | flops 3625254912 | bytes 7864320 | tf_op jit(solution)/shard_map/aik,bkj->aibj/dot_general | solution.py:125
  238.9 4.3 %copy.79 = f32[3,1,256,3,1,256]{5,4,3,2,1,0:T(1,128)} copy(f32[3,1,256,3,1,256]{2,5,0,3,4,1:T(8,128)S(1)} %fusion.27) | data formatting | bytes 4718592 | tf_op jit(solution)/shard_map/scatter | solution.py:135
  (87 shorter events, 21.3 us)
Async XLA Ops:
  6.5 1.1 slice-start
  41.6 25.5 %all-to-all-start.1 = ((f32[16,2,24,256]{3,2,1,0:T(8,128)}), f32[16,2,24,256]{3,2,1,0:T(8,128)S(1)}, u32[]{:S(2)}, u32[]{:S(2)}) async-start(f32[16,2,24,256]{3,2,1,0:T(8,128)} %broadcast_in_dim.75), calls=%async_computation.1 | async-start | bytes 1572864 | tf_op jit(solution)/shard_map/all_to_all | solution.py:62
  50.6 3.4 %copy-start = (f32[3,1,256,3,1,256]{2,5,0,3,4,1:T(8,128)}, f32[3,1,256,3,1,256]{2,5,0,3,4,1:T(8,128)S(1)}, u32[]{:S(2)}) copy-start(f32[3,1,256,3,1,256]{2,5,0,3,4,1:T(8,128)S(1)} %copy.65) | copy-start | bytes 7077892
  67.1 1.1 copy-start.3
  94.4 1.1 copy-start.4
  96.6 23.6 %all-to-all-start.3 = ((f32[16,2,32,256]{3,2,1,0:T(8,128)}), f32[16,2,32,256]{3,2,1,0:T(8,128)S(1)}, u32[]{:S(2)}, u32[]{:S(2)}) async-start(f32[16,2,32,256]{3,2,1,0:T(8,128)} %broadcast_in_dim.76), calls=%async_computation.3 | async-start | bytes 2097152 | tf_op jit(solution)/shard_map/all_to_all | solution.py:81
  100.3 128.5 %all-gather.4.cloned.1.call-start = ((), (), s32[]{:S(2)}) async-start(), calls=%async_computation.4 | async-start | bytes 1671168 | tf_op jit(solution)/shard_map/all_gather | solution.py:89
  120.3 0.7 copy-start.7
  223.3 3.7 %copy-start.2 = (f32[2,768,256]{2,1,0:T(8,128)S(1)}, f32[2,768,256]{2,1,0:T(8,128)}, u32[]{:S(2)}) copy-start(f32[2,768,256]{2,1,0:T(8,128)} %pad_maximum_fusion) | copy-start | bytes 4718596
  231.1 2.3 copy-start.1
  233.4 4.7 %copy-start.5 = (f32[256,256]{0,1:T(8,128)S(1)}, f32[256,256]{0,1:T(8,128)}, u32[]{:S(2)}) copy-start(f32[256,256]{0,1:T(8,128)} %copy.76) | copy-start | bytes 786436
  233.4 4.7 %copy-start.6 = (f32[256,256]{0,1:T(8,128)S(1)}, f32[256,256]{0,1:T(8,128)}, u32[]{:S(2)}) copy-start(f32[256,256]{0,1:T(8,128)} %copy.77) | copy-start | bytes 786436
Sparse Core Ops, SparseCore 0:
  120.3 48.5 all-gather.3
